TPU v7x, 32 devices: a whole 2x2x4 slice. The times are simulated.
32 devices in a mesh: dom: 2 (over y), blk: 16 (over z, x, core).
Axes of the slice: x: 2, y: 2, z: 4, core: 2. Of those that a mesh axis runs over, the one named last changes fastest.
Arguments:
- right_side: float32 [2, 4, 2, 8192], P(None, None, 'dom', 'blk')
- near_blocks: bfloat16 [2, 32, 4, 2, 256, 256], P('dom', 'blk'), may hold values from -0.125 to 0.125
- near_cols: int32 [2, 32, 4], P('dom', 'blk'), may hold values from 0 to 5
- partner: int32 [2, 32], P('dom', 'blk'), may hold values from 0 to 3, as said below
- source_basis: bfloat16 [2, 2, 64, 8192], P('dom', None, None, 'blk'), may hold values from -0.25 to 0.25
- target_basis: bfloat16 [2, 2, 64, 8192], P('dom', None, None, 'blk'), may hold values from -0.75 to 0.75
- coupling: float32 [2, 16, 16, 2, 64, 64], P('dom', 'blk'), as said below
- far_ranks: int32 [2, 16, 16], P('dom', 'blk'), may hold values from 32 to 64, as said below
Outputs:
- second_basis: float32 [2, 4, 2, 8192], P(None, None, 'dom', 'blk')
- third_basis: float32 [2, 4, 2, 8192], P(None, None, 'dom', 'blk')
- hessenberg: float32 [4, 9], replicated
Inputs may be any that keep to these rules, and one draw needn't show every extreme that they name: partner[d, c * 2 + i] = e * 2 + j names block j of cluster c in subdomain e; the named block names the first one back, and no block names itself. coupling[d, c, s, a, k, l] equals coupling[d, s, c, a, l, k]. far_ranks[d, c, s] equals far_ranks[d, s, c].
All inputs are finite; a program needn't handle non-finite values.
Results may differ from a plain program's by a relative error of at most 0.0065.
Values may be sent and summed in bfloat16 or wider, within the bound.
No kernel may reach another device: no remote copies, remote signals or barrier semaphores. Data moves between devices by JAX's collectives and lax.ppermute only.
A program may use at most 64 MiB of HBM per device.

v0:
```python
import jax
import jax.numpy as jnp
from jax import lax
from jax.sharding import PartitionSpec as P

EPSILON = 1e-06


def extended(cells, sides, width):
    for axis, dim in sides:
        count = lax.axis_size(axis)
        ends = count - 1
        head = lax.slice_in_dim(cells, 0, width, axis=dim)
        tail = lax.slice_in_dim(cells, cells.shape[dim] - width, cells.shape[dim], axis=dim)
        cells = jnp.concatenate(
            [
                lax.ppermute(tail, axis, [(i, (i + 1) % count) for i in range(ends)]),
                cells,
                lax.ppermute(head, axis, [((i + 1) % count, i) for i in range(ends)]),
            ],
            axis=dim,
        )
    return cells


def complex_mix(products):
    return jnp.stack([products[0, 0] - products[1, 1], products[0, 1] + products[1, 0]])


def apply_operator(
    vector, near_blocks, near_cols, partner, source_basis, target_basis, coupling, far_ranks
):
    nrhs = vector.shape[1]
    rows = vector.shape[3]
    blocks_dev = near_blocks.shape[1]
    slots = near_blocks.shape[2]
    width = near_blocks.shape[4]
    rank_cap = source_basis.shape[2]
    rounded = vector.astype(jnp.bfloat16)
    window = extended(rounded, (("blk", 3),), rows)
    window = window.reshape(2, nrhs, 3 * blocks_dev, width)
    chosen = jnp.take(window, near_cols[0].reshape(-1), axis=2).reshape(
        2, nrhs, blocks_dev, slots, width
    )
    near_prod = jnp.einsum(
        "ikarc,pqikc->apqir", near_blocks[0], chosen, preferred_element_type=jnp.float32
    )
    near_part = complex_mix(near_prod).reshape(2, nrhs, 1, rows)
    coef_prod = jnp.einsum(
        "akr,pqr->apqk", source_basis[0], rounded[:, :, 0], preferred_element_type=jnp.float32
    )
    coeffs = jnp.stack([coef_prod[0, 0] + coef_prod[1, 1], coef_prod[0, 1] - coef_prod[1, 0]])
    row_coupling = coupling[0, 0]
    row_ranks = far_ranks[0, 0]
    levels = jnp.arange(rank_cap, dtype=jnp.int32)
    limit = row_ranks[:, None, None]
    keep = (levels[None, :, None] < limit) & (levels[None, None, :] < limit)
    weights = row_coupling * keep[:, None].astype(jnp.float32)
    inner = jnp.einsum(
        "sakl,spql->apqk",
        weights,
        lax.all_gather(coeffs[None], "blk", axis=0, tiled=True),
        precision=lax.Precision.HIGHEST,
    )
    far_coef = complex_mix(inner)
    rounded_coef = far_coef.astype(jnp.bfloat16)
    outward = jnp.einsum(
        "akr,pqk->apqr", target_basis[0], rounded_coef, preferred_element_type=jnp.float32
    )
    far_part = complex_mix(outward).reshape(2, nrhs, 1, rows)
    every = lax.all_gather(vector, "dom", axis=2, tiled=True)
    every = every.reshape(2, nrhs, -1, width)
    mates = jnp.take(every, partner[0], axis=2).reshape(2, nrhs, 1, rows)
    return vector + near_part + far_part - mates


def local_products(vectors, image):
    stacked = []
    for basis in vectors:
        real_part = jnp.sum(basis[0] * image[0] + basis[1] * image[1], axis=(1, 2))
        imag_part = jnp.sum(basis[0] * image[1] - basis[1] * image[0], axis=(1, 2))
        stacked.append(jnp.stack([real_part, imag_part]))
    return jnp.stack(stacked)


def local_squares(field):
    return jnp.sum(field[0] * field[0] + field[1] * field[1], axis=(1, 2))


def scaled(factor, field):
    real_f = factor[0][:, None, None]
    imag_f = factor[1][:, None, None]
    return jnp.stack([real_f * field[0] - imag_f * field[1], real_f * field[1] + imag_f * field[0]])


def shards(
    right_side, near_blocks, near_cols, partner, source_basis, target_basis, coupling, far_ranks
):
    rows = right_side.shape[3]
    total = float(rows * lax.axis_size("dom") * lax.axis_size("blk"))

    def operator(field):
        return apply_operator(
            field, near_blocks, near_cols, partner, source_basis, target_basis, coupling, far_ranks
        )

    start_sum = lax.psum(local_squares(right_side), ("dom", "blk"))
    beta = jnp.sqrt(start_sum / total + EPSILON)
    first_vec = right_side / beta[None, :, None, None]
    image_one = operator(first_vec)

    def projections(vectors, image):
        return lax.psum(local_products(vectors, image), ("dom", "blk")) / total

    def lengths(field):
        return lax.psum(local_squares(field), ("dom", "blk")) / total

    h_one_one = projections([first_vec], image_one)[0]
    rest_one = image_one - scaled(h_one_one, first_vec)
    h_two_one = jnp.sqrt(lengths(rest_one) + EPSILON)
    second_basis = rest_one / h_two_one[None, :, None, None]
    image_two = operator(second_basis)
    both = projections([first_vec, second_basis], image_two)
    h_one_two = both[0]
    h_two_two = both[1]
    rest_two = image_two - scaled(h_one_two, first_vec) - scaled(h_two_two, second_basis)
    h_three_two = jnp.sqrt(lengths(rest_two) + EPSILON)
    third_basis = rest_two / h_three_two[None, :, None, None]
    hessenberg = jnp.stack(
        [
            beta,
            h_one_one[0],
            h_one_one[1],
            h_two_one,
            h_one_two[0],
            h_one_two[1],
            h_two_two[0],
            h_two_two[1],
            h_three_two,
        ],
        axis=1,
    )
    return (second_basis, third_basis, hessenberg)


def solution(mesh):
    return jax.shard_map(
        shards,
        mesh=mesh,
        in_specs=(
            P(None, None, "dom", "blk"),
            P("dom", "blk", None, None, None, None),
            P("dom", "blk", None),
            P("dom", "blk"),
            P("dom", None, None, "blk"),
            P("dom", None, None, "blk"),
            P("dom", "blk", None, None, None, None),
            P("dom", "blk", None),
        ),
        out_specs=(P(None, None, "dom", "blk"), P(None, None, "dom", "blk"), P()),
        check_vma=False,
    )
```

profile of v0, /device:TPU:0, one launch (start us, length us, event | category | flops | bytes accessed | tf_op | source)
XLA Modules:
  0.0 278.6 jit_solution(17837477689193010791)
XLA Ops:
  0.7 1.0 add_reduce_fusion.3
  1.7 42.0 %psum.35 = f32[4]{0:T(128)S(1)} all-reduce(f32[4]{0:T(128)S(1)} %add_reduce_fusion.3), channel_id=1, replica_groups=mesh['dom'=2,'blk'=16] {'dom','blk'}, use_global_device_ids=true, to_apply=%region_1.0 | all-reduce | flops 4 | bytes 32 | tf_op jit(solution)/shard_map/psum | solution.py:107
  43.7 0.8 fusion.64
  44.5 1.3 collective-permute-start
  45.8 1.3 collective-permute-start.1
  47.1 1.1 convolution_bitcast_fusion.3
  48.2 24.1 %all-gather = f32[32,4,64]{2,1,0:T(4,128)S(1)} all-gather(f32[2,4,64]{2,1,0:T(4,128)S(1)} %pad_maximum_fusion.2), channel_id=2, replica_groups=mesh['dom'=2,'blk'=16] {'blk'}, dimensions={0}, use_global_device_ids=true | all-gather | bytes 34816 | tf_op jit(solution)/shard_map/all_gather | solution.py:62
  72.3 0.7 iota_compare_fusion
  73.2 2.6 fusion.12
  76.2 4.4 %all_gather.13 = f32[2,4,2,512]{3,1,0,2:T(4,128)S(1)} all-gather(f32[2,4,1,512]{3,1,0,2:T(4,128)S(1)} %get-tuple-element.28), channel_id=1, replica_groups=mesh['dom'=2,'blk'=16] {'dom'}, dimensions={2}, use_global_device_ids=true | all-gather | bytes 49152 | tf_op jit(solution)/shard_map/all_gather | solution.py:71
  82.2 0.7 fusion.4
  83.1 36.9 %psum.36 = f32[1,2,4]{2,1,0:T(2,128)S(1)} all-reduce(f32[1,2,4]{2,1,0:T(2,128)S(1)} %maximum_bitcast_fusion.6), channel_id=1, replica_groups=mesh['dom'=2,'blk'=16] {'dom','blk'}, use_global_device_ids=true, to_apply=%region_4.7 | all-reduce | flops 8 | bytes 64 | tf_op jit(solution)/shard_map/psum | solution.py:113
  120.3 41.3 %psum.37 = f32[4]{0:T(128)S(1)} all-reduce(f32[4]{0:T(128)S(1)} %fusion.34), channel_id=1, replica_groups=mesh['dom'=2,'blk'=16] {'dom','blk'}, use_global_device_ids=true, to_apply=%region_6.9 | all-reduce | flops 4 | bytes 32 | tf_op jit(solution)/shard_map/psum | solution.py:116
  161.9 20.6 %all-gather.1 = f32[32,4,64]{2,1,0:T(4,128)S(1)} all-gather(f32[2,4,64]{2,1,0:T(4,128)S(1)} %pad_maximum_fusion.3), channel_id=3, replica_groups=mesh['dom'=2,'blk'=16] {'blk'}, dimensions={0}, use_global_device_ids=true | all-gather | bytes 34816 | tf_op jit(solution)/shard_map/all_gather | solution.py:62
  182.5 2.6 fusion.10
  185.1 2.2 collective-permute-start.2
  187.4 1.3 collective-permute-start.3
  188.7 4.4 %all_gather.15 = f32[2,4,2,512]{3,1,0,2:T(4,128)S(1)} all-gather(f32[2,4,1,512]{3,1,0,2:T(4,128)S(1)} %get-tuple-element.26), channel_id=1, replica_groups=mesh['dom'=2,'blk'=16] {'dom'}, dimensions={2}, use_global_device_ids=true | all-gather | bytes 49152 | tf_op jit(solution)/shard_map/all_gather | solution.py:71
  194.0 0.6 copy.145
  195.5 0.7 fusion.7
  196.5 39.3 %psum.38 = f32[2,2,4]{2,1,0:T(2,128)S(1)} all-reduce(f32[2,2,4]{2,1,0:T(2,128)S(1)} %pad_maximum_fusion.4), channel_id=1, replica_groups=mesh['dom'=2,'blk'=16] {'dom','blk'}, use_global_device_ids=true, to_apply=%region_11.14 | all-reduce | flops 16 | bytes 128 | tf_op jit(solution)/shard_map/psum | solution.py:113
  236.2 40.5 %psum.39 = f32[4]{0:T(128)S(1)} all-reduce(f32[4]{0:T(128)S(1)} %fusion.30), channel_id=1, replica_groups=mesh['dom'=2,'blk'=16] {'dom','blk'}, use_global_device_ids=true, to_apply=%region_13.16 | all-reduce | flops 4 | bytes 32 | tf_op jit(solution)/shard_map/psum | solution.py:116
  277.3 0.6 copy.146
  277.9 0.7 stack.135
  (96 shorter events, 5.7 us)
Async XLA Ops:
  0.6 81.5 %copy-start = (bf16[1,2,4,2,256,256]{5,4,3,2,1,0:T(8,128)(2,1)S(1)}, bf16[1,2,4,2,256,256]{5,4,3,2,1,0:T(8,128)(2,1)}, u32[]{:S(2)}) copy-start(bf16[1,2,4,2,256,256]{5,4,3,2,1,0:T(8,128)(2,1)} %param.13) | copy-start | bytes 6291460
  0.6 75.3 %copy-start.2 = (bf16[1,2,64,512]{3,2,1,0:T(8,128)(2,1)S(1)}, bf16[1,2,64,512]{3,2,1,0:T(8,128)(2,1)}, u32[]{:S(2)}) copy-start(bf16[1,2,64,512]{3,2,1,0:T(8,128)(2,1)} %param.17) | copy-start | bytes 393220
  0.7 75.4 %copy-start.3 = (s32[1,2,4]{2,1,0:T(2,128)S(1)}, s32[1,2,4]{2,1,0:T(2,128)}, u32[]{:S(2)}) copy-start(s32[1,2,4]{2,1,0:T(2,128)} %param.14) | copy-start | bytes 100
  0.7 75.5 %copy-start.4 = (s32[1,2]{1,0:T(1,128)S(1)}, s32[1,2]{1,0:T(1,128)}, u32[]{:S(2)}) copy-start(s32[1,2]{1,0:T(1,128)} %param.15) | copy-start | bytes 28
  44.5 37.0 %collective-permute-start = (bf16[2,4,1,512]{3,1,0,2:T(4,128)(2,1)S(1)}, bf16[2,4,1,512]{3,1,0,2:T(4,128)(2,1)S(1)}, u32[]{:S(2)}, u32[]{:S(2)}) collective-permute-start(bf16[2,4,1,512]{3,1,0,2:T(4,128)(2,1)S(1)} %get-tuple-element.27), channel_id=1, source_target_pairs={{0,1},{1,2},{2,3},{3,4},{4,5},{5,6},{6,7},{7,8},{8,9},{9,10},{10,1... | collective-permute-start | bytes 24584 | tf_op jit(solution)/shard_map/ppermute | solution.py:17
  45.8 35.7 %collective-permute-start.1 = (bf16[2,4,1,512]{3,1,0,2:T(4,128)(2,1)S(1)}, bf16[2,4,1,512]{3,1,0,2:T(4,128)(2,1)S(1)}, u32[]{:S(2)}, u32[]{:S(2)}) collective-permute-start(bf16[2,4,1,512]{3,1,0,2:T(4,128)(2,1)S(1)} %get-tuple-element.27), channel_id=1, source_target_pairs={{1,0},{2,1},{3,2},{4,3},{5,4},{6,5},{7,6},{8,7},{9,8},{10,9},{11,1... | collective-permute-start | bytes 24584 | tf_op jit(solution)/shard_map/ppermute | solution.py:19
  75.9 85.8 %copy-start.1 = (bf16[1,2,64,512]{3,2,1,0:T(8,128)(2,1)S(1)}, bf16[1,2,64,512]{3,2,1,0:T(8,128)(2,1)}, u32[]{:S(2)}) copy-start(bf16[1,2,64,512]{3,2,1,0:T(8,128)(2,1)} %param.16) | copy-start | bytes 393220
  185.1 9.7 %collective-permute-start.2 = (bf16[2,4,1,512]{3,1,0,2:T(4,128)(2,1)S(1)}, bf16[2,4,1,512]{3,1,0,2:T(4,128)(2,1)S(1)}, u32[]{:S(2)}, u32[]{:S(2)}) collective-permute-start(bf16[2,4,1,512]{3,1,0,2:T(4,128)(2,1)S(1)} %get-tuple-element.25), channel_id=1, source_target_pairs={{0,1},{1,2},{2,3},{3,4},{4,5},{5,6},{6,7},{7,8},{8,9},{9,10},{10,1... | collective-permute-start | bytes 24584 | tf_op jit(solution)/shard_map/ppermute | solution.py:17
  187.4 7.4 %collective-permute-start.3 = (bf16[2,4,1,512]{3,1,0,2:T(4,128)(2,1)S(1)}, bf16[2,4,1,512]{3,1,0,2:T(4,128)(2,1)S(1)}, u32[]{:S(2)}, u32[]{:S(2)}) collective-permute-start(bf16[2,4,1,512]{3,1,0,2:T(4,128)(2,1)S(1)} %get-tuple-element.25), channel_id=1, source_target_pairs={{1,0},{2,1},{3,2},{4,3},{5,4},{6,5},{7,6},{8,7},{9,8},{10,9},{11,1... | collective-permute-start | bytes 24584 | tf_op jit(solution)/shard_map/ppermute | solution.py:19
where the time goes:
time: 280 us; the launch traced here: 279 us
  blocking collectives  254 us (91%)
  matrix products  8.05 us (3%)
  starting transfers between devices  6.11 us (2%)
  local copies, waits for them, and re-layouts  5.44 us (2%)
  other arithmetic  4.26 us (2%)
    psum x2, blocking collectives, lengths(): return lax.psum(local_squares(field), ('dom', 'blk')) / total  81.9 us
    psum x2, blocking collectives, projections(): return lax.psum(local_products(vectors, image), ('dom', 'blk')) / total  76.2 us
    all_gather x2, blocking collectives, apply_operator(): lax.all_gather(coeffs[None], 'blk', axis=0, tiled=True)  44.7 us
    psum x1, blocking collectives, shards(): start_sum = lax.psum(local_squares(right_side), ('dom', 'blk'))  42 us
    all_gather x2, blocking collectives, apply_operator(): every = lax.all_gather(vector, 'dom', axis=2, tiled=True)  8.85 us
  transfers between devices with their start and end apart: 4, of which 0 were waited for; matrix products, arithmetic and copies ran while one was open for 3% of the time, Pallas kernels for 0%

commit v1 on v0

--- a/solution.py
+++ b/solution.py
@@ -56,12 +56,26 @@
     limit = row_ranks[:, None, None]
     keep = (levels[None, :, None] < limit) & (levels[None, None, :] < limit)
     weights = row_coupling * keep[:, None].astype(jnp.float32)
+    devices, index = (lax.axis_size("blk"), lax.axis_index("blk"))
+    backward = [(i_2, (i_2 - 1) % devices) for i_2 in range(devices)]
+    span = coeffs[None].shape[0]
+    held = coeffs[None]
     inner = jnp.einsum(
         "sakl,spql->apqk",
-        weights,
-        lax.all_gather(coeffs[None], "blk", axis=0, tiled=True),
+        lax.dynamic_slice_in_dim(weights, index * span, held.shape[0], axis=0),
+        held,
         precision=lax.Precision.HIGHEST,
     )
+    for step in range(1, devices):
+        held = lax.ppermute(held, "blk", backward)
+        inner = inner + jnp.einsum(
+            "sakl,spql->apqk",
+            lax.dynamic_slice_in_dim(
+                weights, (index + step) % devices * span, held.shape[0], axis=0
+            ),
+            held,
+            precision=lax.Precision.HIGHEST,
+        )
     far_coef = complex_mix(inner)
     rounded_coef = far_coef.astype(jnp.bfloat16)
     outward = jnp.einsum(

time: 280 us -> 395 us (1.41)
  starting transfers between devices: 6.11 us -> 130 us
  blocking collectives: 254 us -> 210 us
  waiting for transfers between devices: 0.01 us -> 27.9 us
    ppermute x0 -> x30, starting transfers between devices: none -> 124 us  [apply_operator(): held = lax.ppermute(held, 'blk', backward)]
    all_gather x2 -> x0, blocking collectives: 44.7 us -> none  [apply_operator(): lax.all_gather(coeffs[None], 'blk', axis=0, tiled=True)]
    ppermute x0 -> x30, waiting for transfers between devices: none -> 27.9 us  [apply_operator(): held = lax.ppermute(held, 'blk', backward)]
    dot_general x2 -> x32, matrix products: 5.25 us -> 8.14 us  [the longest x30 7.63 us: apply_operator(): jnp.einsum('sakl,spql->apqk', lax.dynamic_slice_in_dim(weights, (index +...]
  transfers between devices with their start and end apart: 4 -> 34, of which waited for: 0 -> 26; matrix products, arithmetic and copies ran while one was open for 3% -> 5% of each run, Pallas kernels for 0% -> 0%
where the time goes in v1:
time: 395 us; the launch traced here: 394 us
  blocking collectives  210 us (53%)
  starting transfers between devices  130 us (33%)
  waiting for transfers between devices  27.9 us (7%)
  matrix products  10.9 us (3%)
  other arithmetic  7.86 us (2%)
  local copies, waits for them, and re-layouts  6.14 us (2%)
    ppermute x30, starting transfers between devices, apply_operator(): held = lax.ppermute(held, 'blk', backward)  124 us
    psum x2, blocking collectives, lengths(): return lax.psum(local_squares(field), ('dom', 'blk')) / total  82.1 us
    psum x2, blocking collectives, projections(): return lax.psum(local_products(vectors, image), ('dom', 'blk')) / total  77.4 us
    psum x1, blocking collectives, shards(): start_sum = lax.psum(local_squares(right_side), ('dom', 'blk'))  42 us
    ppermute x30, waiting for transfers between devices, apply_operator(): held = lax.ppermute(held, 'blk', backward)  27.9 us
    all_gather x2, blocking collectives, apply_operator(): every = lax.all_gather(vector, 'dom', axis=2, tiled=True)  8.81 us
  transfers between devices with their start and end apart: 34, of which 26 were waited for; matrix products, arithmetic and copies ran while one was open for 5% of the time, Pallas kernels for 0%

profile of v1, /device:TPU:0, one launch (start us, length us, event | category | flops | bytes accessed | tf_op | source)
XLA Modules:
  0.0 393.9 jit_solution(4930439934897269310)
XLA Ops:
  1.6 42.0 %psum.35 = f32[4]{0:T(128)S(1)} all-reduce(f32[4]{0:T(128)S(1)} %add_reduce_fusion.3), channel_id=1, replica_groups=mesh['dom'=2,'blk'=16] {'dom','blk'}, use_global_device_ids=true, to_apply=%region_1.0 | all-reduce | flops 4 | bytes 32 | tf_op jit(solution)/shard_map/psum | solution.py:121
  48.1 5.3 %collective-permute-start.2 = (f32[1,2,4,64]{3,2,1,0:T(4,128)S(1)}, f32[1,2,4,64]{3,2,1,0:T(4,128)S(1)}, u32[]{:S(2)}, u32[]{:S(2)}) collective-permute-start(f32[1,2,4,64]{3,2,1,0:T(4,128)S(1)} %fusion.165), channel_id=1, source_target_pairs={{0,15},{1,0},{2,1},{3,2},{4,3},{5,4},{6,5},{7,6},{8,7},{9,8},{10,9... | collective-permute-start | bytes 6152 | tf_op jit(solution)/shard_map/ppermute | solution.py:70
  57.3 4.4 %all_gather.6 = f32[2,4,2,512]{3,1,0,2:T(4,128)S(1)} all-gather(f32[2,4,1,512]{3,1,0,2:T(4,128)S(1)} %get-tuple-element.25), channel_id=1, replica_groups=mesh['dom'=2,'blk'=16] {'dom'}, dimensions={2}, use_global_device_ids=true | all-gather | bytes 49152 | tf_op jit(solution)/shard_map/all_gather | solution.py:85
  66.3 4.4 %collective-permute-start.4 = (f32[1,2,4,64]{3,2,1,0:T(4,128)S(1)}, f32[1,2,4,64]{3,2,1,0:T(4,128)S(1)}, u32[]{:S(2)}, u32[]{:S(2)}) collective-permute-start(f32[1,2,4,64]{3,2,1,0:T(4,128)S(1)} %collective-permute-done.3), channel_id=1, source_target_pairs={{0,15},{1,0},{2,1},{3,2},{4,3},{5,4},{6,5},{7,6},{8,7},{9,8},{10,9... | collective-permute-start | bytes 6152 | tf_op jit(solution)/shard_map/ppermute | solution.py:70
  72.0 4.4 %collective-permute-start.5 = (f32[1,2,4,64]{3,2,1,0:T(4,128)S(1)}, f32[1,2,4,64]{3,2,1,0:T(4,128)S(1)}, u32[]{:S(2)}, u32[]{:S(2)}) collective-permute-start(f32[1,2,4,64]{3,2,1,0:T(4,128)S(1)} %collective-permute-done.4), channel_id=1, source_target_pairs={{0,15},{1,0},{2,1},{3,2},{4,3},{5,4},{6,5},{7,6},{8,7},{9,8},{10,9... | collective-permute-start | bytes 6152 | tf_op jit(solution)/shard_map/ppermute | solution.py:70
  83.5 4.4 %collective-permute-start.7 = (f32[1,2,4,64]{3,2,1,0:T(4,128)S(1)}, f32[1,2,4,64]{3,2,1,0:T(4,128)S(1)}, u32[]{:S(2)}, u32[]{:S(2)}) collective-permute-start(f32[1,2,4,64]{3,2,1,0:T(4,128)S(1)} %collective-permute-done.6), channel_id=1, source_target_pairs={{0,15},{1,0},{2,1},{3,2},{4,3},{5,4},{6,5},{7,6},{8,7},{9,8},{10,9... | collective-permute-start | bytes 6152 | tf_op jit(solution)/shard_map/ppermute | solution.py:70
  89.2 4.4 %collective-permute-start.8 = (f32[1,2,4,64]{3,2,1,0:T(4,128)S(1)}, f32[1,2,4,64]{3,2,1,0:T(4,128)S(1)}, u32[]{:S(2)}, u32[]{:S(2)}) collective-permute-start(f32[1,2,4,64]{3,2,1,0:T(4,128)S(1)} %collective-permute-done.7), channel_id=1, source_target_pairs={{0,15},{1,0},{2,1},{3,2},{4,3},{5,4},{6,5},{7,6},{8,7},{9,8},{10,9... | collective-permute-start | bytes 6152 | tf_op jit(solution)/shard_map/ppermute | solution.py:70
  95.0 4.4 %collective-permute-start.9 = (f32[1,2,4,64]{3,2,1,0:T(4,128)S(1)}, f32[1,2,4,64]{3,2,1,0:T(4,128)S(1)}, u32[]{:S(2)}, u32[]{:S(2)}) collective-permute-start(f32[1,2,4,64]{3,2,1,0:T(4,128)S(1)} %collective-permute-done.8), channel_id=1, source_target_pairs={{0,15},{1,0},{2,1},{3,2},{4,3},{5,4},{6,5},{7,6},{8,7},{9,8},{10,9... | collective-permute-start | bytes 6152 | tf_op jit(solution)/shard_map/ppermute | solution.py:70
  100.7 4.4 %collective-permute-start.10 = (f32[1,2,4,64]{3,2,1,0:T(4,128)S(1)}, f32[1,2,4,64]{3,2,1,0:T(4,128)S(1)}, u32[]{:S(2)}, u32[]{:S(2)}) collective-permute-start(f32[1,2,4,64]{3,2,1,0:T(4,128)S(1)} %collective-permute-done.9), channel_id=1, source_target_pairs={{0,15},{1,0},{2,1},{3,2},{4,3},{5,4},{6,5},{7,6},{8,7},{9,8},{10,9... | collective-permute-start | bytes 6152 | tf_op jit(solution)/shard_map/ppermute | solution.py:70
  106.4 4.4 %collective-permute-start.11 = (f32[1,2,4,64]{3,2,1,0:T(4,128)S(1)}, f32[1,2,4,64]{3,2,1,0:T(4,128)S(1)}, u32[]{:S(2)}, u32[]{:S(2)}) collective-permute-start(f32[1,2,4,64]{3,2,1,0:T(4,128)S(1)} %collective-permute-done.10), channel_id=1, source_target_pairs={{0,15},{1,0},{2,1},{3,2},{4,3},{5,4},{6,5},{7,6},{8,7},{9,8},{10,9... | collective-permute-start | bytes 6152 | tf_op jit(solution)/shard_map/ppermute | solution.py:70
  112.1 4.4 %collective-permute-start.12 = (f32[1,2,4,64]{3,2,1,0:T(4,128)S(1)}, f32[1,2,4,64]{3,2,1,0:T(4,128)S(1)}, u32[]{:S(2)}, u32[]{:S(2)}) collective-permute-start(f32[1,2,4,64]{3,2,1,0:T(4,128)S(1)} %collective-permute-done.11), channel_id=1, source_target_pairs={{0,15},{1,0},{2,1},{3,2},{4,3},{5,4},{6,5},{7,6},{8,7},{9,8},{10,9... | collective-permute-start | bytes 6152 | tf_op jit(solution)/shard_map/ppermute | solution.py:70
  117.9 4.4 %collective-permute-start.13 = (f32[1,2,4,64]{3,2,1,0:T(4,128)S(1)}, f32[1,2,4,64]{3,2,1,0:T(4,128)S(1)}, u32[]{:S(2)}, u32[]{:S(2)}) collective-permute-start(f32[1,2,4,64]{3,2,1,0:T(4,128)S(1)} %collective-permute-done.12), channel_id=1, source_target_pairs={{0,15},{1,0},{2,1},{3,2},{4,3},{5,4},{6,5},{7,6},{8,7},{9,8},{10,9... | collective-permute-start | bytes 6152 | tf_op jit(solution)/shard_map/ppermute | solution.py:70
  123.6 4.4 %collective-permute-start.14 = (f32[1,2,4,64]{3,2,1,0:T(4,128)S(1)}, f32[1,2,4,64]{3,2,1,0:T(4,128)S(1)}, u32[]{:S(2)}, u32[]{:S(2)}) collective-permute-start(f32[1,2,4,64]{3,2,1,0:T(4,128)S(1)} %collective-permute-done.13), channel_id=1, source_target_pairs={{0,15},{1,0},{2,1},{3,2},{4,3},{5,4},{6,5},{7,6},{8,7},{9,8},{10,9... | collective-permute-start | bytes 6152 | tf_op jit(solution)/shard_map/ppermute | solution.py:70
  129.3 4.4 %collective-permute-start.15 = (f32[1,2,4,64]{3,2,1,0:T(4,128)S(1)}, f32[1,2,4,64]{3,2,1,0:T(4,128)S(1)}, u32[]{:S(2)}, u32[]{:S(2)}) collective-permute-start(f32[1,2,4,64]{3,2,1,0:T(4,128)S(1)} %collective-permute-done.14), channel_id=1, source_target_pairs={{0,15},{1,0},{2,1},{3,2},{4,3},{5,4},{6,5},{7,6},{8,7},{9,8},{10,9... | collective-permute-start | bytes 6152 | tf_op jit(solution)/shard_map/ppermute | solution.py:70
  135.1 4.4 %collective-permute-start.16 = (f32[1,2,4,64]{3,2,1,0:T(4,128)S(1)}, f32[1,2,4,64]{3,2,1,0:T(4,128)S(1)}, u32[]{:S(2)}, u32[]{:S(2)}) collective-permute-start(f32[1,2,4,64]{3,2,1,0:T(4,128)S(1)} %collective-permute-done.15), channel_id=1, source_target_pairs={{0,15},{1,0},{2,1},{3,2},{4,3},{5,4},{6,5},{7,6},{8,7},{9,8},{10,9... | collective-permute-start | bytes 6152 | tf_op jit(solution)/shard_map/ppermute | solution.py:70
  141.4 38.7 %psum.36 = f32[1,2,4]{2,1,0:T(2,128)S(1)} all-reduce(f32[1,2,4]{2,1,0:T(2,128)S(1)} %maximum_bitcast_fusion.6), channel_id=1, replica_groups=mesh['dom'=2,'blk'=16] {'dom','blk'}, use_global_device_ids=true, to_apply=%region_4.7 | all-reduce | flops 8 | bytes 64 | tf_op jit(solution)/shard_map/psum | solution.py:127
  180.4 40.7 %psum.37 = f32[4]{0:T(128)S(1)} all-reduce(f32[4]{0:T(128)S(1)} %fusion.94), channel_id=1, replica_groups=mesh['dom'=2,'blk'=16] {'dom','blk'}, use_global_device_ids=true, to_apply=%region_6.9 | all-reduce | flops 4 | bytes 32 | tf_op jit(solution)/shard_map/psum | solution.py:130
  222.7 4.7 %collective-permute-start.19 = (f32[1,2,4,64]{3,2,1,0:T(4,128)S(1)}, f32[1,2,4,64]{3,2,1,0:T(4,128)S(1)}, u32[]{:S(2)}, u32[]{:S(2)}) collective-permute-start(f32[1,2,4,64]{3,2,1,0:T(4,128)S(1)} %fusion.164), channel_id=1, source_target_pairs={{0,15},{1,0},{2,1},{3,2},{4,3},{5,4},{6,5},{7,6},{8,7},{9,8},{10,9... | collective-permute-start | bytes 6152 | tf_op jit(solution)/shard_map/ppermute | solution.py:70
  227.4 4.4 %all_gather.7 = f32[2,4,2,512]{3,1,0,2:T(4,128)S(1)} all-gather(f32[2,4,1,512]{3,1,0,2:T(4,128)S(1)} %get-tuple-element.23), channel_id=1, replica_groups=mesh['dom'=2,'blk'=16] {'dom'}, dimensions={2}, use_global_device_ids=true | all-gather | bytes 49152 | tf_op jit(solution)/shard_map/all_gather | solution.py:85
  236.2 4.4 %collective-permute-start.21 = (f32[1,2,4,64]{3,2,1,0:T(4,128)S(1)}, f32[1,2,4,64]{3,2,1,0:T(4,128)S(1)}, u32[]{:S(2)}, u32[]{:S(2)}) collective-permute-start(f32[1,2,4,64]{3,2,1,0:T(4,128)S(1)} %collective-permute-done.20), channel_id=1, source_target_pairs={{0,15},{1,0},{2,1},{3,2},{4,3},{5,4},{6,5},{7,6},{8,7},{9,8},{10,9... | collective-permute-start | bytes 6152 | tf_op jit(solution)/shard_map/ppermute | solution.py:70
  242.0 4.4 %collective-permute-start.22 = (f32[1,2,4,64]{3,2,1,0:T(4,128)S(1)}, f32[1,2,4,64]{3,2,1,0:T(4,128)S(1)}, u32[]{:S(2)}, u32[]{:S(2)}) collective-permute-start(f32[1,2,4,64]{3,2,1,0:T(4,128)S(1)} %collective-permute-done.21), channel_id=1, source_target_pairs={{0,15},{1,0},{2,1},{3,2},{4,3},{5,4},{6,5},{7,6},{8,7},{9,8},{10,9... | collective-permute-start | bytes 6152 | tf_op jit(solution)/shard_map/ppermute | solution.py:70
  253.4 4.4 %collective-permute-start.24 = (f32[1,2,4,64]{3,2,1,0:T(4,128)S(1)}, f32[1,2,4,64]{3,2,1,0:T(4,128)S(1)}, u32[]{:S(2)}, u32[]{:S(2)}) collective-permute-start(f32[1,2,4,64]{3,2,1,0:T(4,128)S(1)} %collective-permute-done.23), channel_id=1, source_target_pairs={{0,15},{1,0},{2,1},{3,2},{4,3},{5,4},{6,5},{7,6},{8,7},{9,8},{10,9... | collective-permute-start | bytes 6152 | tf_op jit(solution)/shard_map/ppermute | solution.py:70
  311.5 38.7 %psum.38 = f32[2,2,4]{2,1,0:T(2,128)S(1)} all-reduce(f32[2,2,4]{2,1,0:T(2,128)S(1)} %pad_maximum_fusion.6), channel_id=1, replica_groups=mesh['dom'=2,'blk'=16] {'dom','blk'}, use_global_device_ids=true, to_apply=%region_11.14 | all-reduce | flops 16 | bytes 128 | tf_op jit(solution)/shard_map/psum | solution.py:127
  350.6 41.4 %psum.39 = f32[4]{0:T(128)S(1)} all-reduce(f32[4]{0:T(128)S(1)} %fusion.90), channel_id=1, replica_groups=mesh['dom'=2,'blk'=16] {'dom','blk'}, use_global_device_ids=true, to_apply=%region_13.16 | all-reduce | flops 4 | bytes 32 | tf_op jit(solution)/shard_map/psum | solution.py:130
  (177 shorter events, 106.4 us)
Async XLA Ops:
  44.4 32.3 %collective-permute-start = (bf16[2,4,1,512]{3,1,0,2:T(4,128)(2,1)S(1)}, bf16[2,4,1,512]{3,1,0,2:T(4,128)(2,1)S(1)}, u32[]{:S(2)}, u32[]{:S(2)}) collective-permute-start(bf16[2,4,1,512]{3,1,0,2:T(4,128)(2,1)S(1)} %get-tuple-element.24), channel_id=1, source_target_pairs={{0,1},{1,2},{2,3},{3,4},{4,5},{5,6},{6,7},{7,8},{8,9},{9,10},{10,1... | collective-permute-start | bytes 24584 | tf_op jit(solution)/shard_map/ppermute | solution.py:17
  45.7 31.0 %collective-permute-start.1 = (bf16[2,4,1,512]{3,1,0,2:T(4,128)(2,1)S(1)}, bf16[2,4,1,512]{3,1,0,2:T(4,128)(2,1)S(1)}, u32[]{:S(2)}, u32[]{:S(2)}) collective-permute-start(bf16[2,4,1,512]{3,1,0,2:T(4,128)(2,1)S(1)} %get-tuple-element.24), channel_id=1, source_target_pairs={{1,0},{2,1},{3,2},{4,3},{5,4},{6,5},{7,6},{8,7},{9,8},{10,9},{11,1... | collective-permute-start | bytes 24584 | tf_op jit(solution)/shard_map/ppermute | solution.py:19
  48.1 16.2 %collective-permute-start.2 = (f32[1,2,4,64]{3,2,1,0:T(4,128)S(1)}, f32[1,2,4,64]{3,2,1,0:T(4,128)S(1)}, u32[]{:S(2)}, u32[]{:S(2)}) collective-permute-start(f32[1,2,4,64]{3,2,1,0:T(4,128)S(1)} %fusion.165), channel_id=1, source_target_pairs={{0,15},{1,0},{2,1},{3,2},{4,3},{5,4},{6,5},{7,6},{8,7},{9,8},{10,9... | collective-permute-start | bytes 6152 | tf_op jit(solution)/shard_map/ppermute | solution.py:70
  66.3 5.7 %collective-permute-start.4 = (f32[1,2,4,64]{3,2,1,0:T(4,128)S(1)}, f32[1,2,4,64]{3,2,1,0:T(4,128)S(1)}, u32[]{:S(2)}, u32[]{:S(2)}) collective-permute-start(f32[1,2,4,64]{3,2,1,0:T(4,128)S(1)} %collective-permute-done.3), channel_id=1, source_target_pairs={{0,15},{1,0},{2,1},{3,2},{4,3},{5,4},{6,5},{7,6},{8,7},{9,8},{10,9... | collective-permute-start | bytes 6152 | tf_op jit(solution)/shard_map/ppermute | solution.py:70
  72.0 6.1 %collective-permute-start.5 = (f32[1,2,4,64]{3,2,1,0:T(4,128)S(1)}, f32[1,2,4,64]{3,2,1,0:T(4,128)S(1)}, u32[]{:S(2)}, u32[]{:S(2)}) collective-permute-start(f32[1,2,4,64]{3,2,1,0:T(4,128)S(1)} %collective-permute-done.4), channel_id=1, source_target_pairs={{0,15},{1,0},{2,1},{3,2},{4,3},{5,4},{6,5},{7,6},{8,7},{9,8},{10,9... | collective-permute-start | bytes 6152 | tf_op jit(solution)/shard_map/ppermute | solution.py:70
  83.5 5.7 %collective-permute-start.7 = (f32[1,2,4,64]{3,2,1,0:T(4,128)S(1)}, f32[1,2,4,64]{3,2,1,0:T(4,128)S(1)}, u32[]{:S(2)}, u32[]{:S(2)}) collective-permute-start(f32[1,2,4,64]{3,2,1,0:T(4,128)S(1)} %collective-permute-done.6), channel_id=1, source_target_pairs={{0,15},{1,0},{2,1},{3,2},{4,3},{5,4},{6,5},{7,6},{8,7},{9,8},{10,9... | collective-permute-start | bytes 6152 | tf_op jit(solution)/shard_map/ppermute | solution.py:70
  89.2 5.7 %collective-permute-start.8 = (f32[1,2,4,64]{3,2,1,0:T(4,128)S(1)}, f32[1,2,4,64]{3,2,1,0:T(4,128)S(1)}, u32[]{:S(2)}, u32[]{:S(2)}) collective-permute-start(f32[1,2,4,64]{3,2,1,0:T(4,128)S(1)} %collective-permute-done.7), channel_id=1, source_target_pairs={{0,15},{1,0},{2,1},{3,2},{4,3},{5,4},{6,5},{7,6},{8,7},{9,8},{10,9... | collective-permute-start | bytes 6152 | tf_op jit(solution)/shard_map/ppermute | solution.py:70
  95.0 5.7 %collective-permute-start.9 = (f32[1,2,4,64]{3,2,1,0:T(4,128)S(1)}, f32[1,2,4,64]{3,2,1,0:T(4,128)S(1)}, u32[]{:S(2)}, u32[]{:S(2)}) collective-permute-start(f32[1,2,4,64]{3,2,1,0:T(4,128)S(1)} %collective-permute-done.8), channel_id=1, source_target_pairs={{0,15},{1,0},{2,1},{3,2},{4,3},{5,4},{6,5},{7,6},{8,7},{9,8},{10,9... | collective-permute-start | bytes 6152 | tf_op jit(solution)/shard_map/ppermute | solution.py:70
  100.7 5.7 %collective-permute-start.10 = (f32[1,2,4,64]{3,2,1,0:T(4,128)S(1)}, f32[1,2,4,64]{3,2,1,0:T(4,128)S(1)}, u32[]{:S(2)}, u32[]{:S(2)}) collective-permute-start(f32[1,2,4,64]{3,2,1,0:T(4,128)S(1)} %collective-permute-done.9), channel_id=1, source_target_pairs={{0,15},{1,0},{2,1},{3,2},{4,3},{5,4},{6,5},{7,6},{8,7},{9,8},{10,9... | collective-permute-start | bytes 6152 | tf_op jit(solution)/shard_map/ppermute | solution.py:70
  106.4 5.7 %collective-permute-start.11 = (f32[1,2,4,64]{3,2,1,0:T(4,128)S(1)}, f32[1,2,4,64]{3,2,1,0:T(4,128)S(1)}, u32[]{:S(2)}, u32[]{:S(2)}) collective-permute-start(f32[1,2,4,64]{3,2,1,0:T(4,128)S(1)} %collective-permute-done.10), channel_id=1, source_target_pairs={{0,15},{1,0},{2,1},{3,2},{4,3},{5,4},{6,5},{7,6},{8,7},{9,8},{10,9... | collective-permute-start | bytes 6152 | tf_op jit(solution)/shard_map/ppermute | solution.py:70
  112.1 5.7 %collective-permute-start.12 = (f32[1,2,4,64]{3,2,1,0:T(4,128)S(1)}, f32[1,2,4,64]{3,2,1,0:T(4,128)S(1)}, u32[]{:S(2)}, u32[]{:S(2)}) collective-permute-start(f32[1,2,4,64]{3,2,1,0:T(4,128)S(1)} %collective-permute-done.11), channel_id=1, source_target_pairs={{0,15},{1,0},{2,1},{3,2},{4,3},{5,4},{6,5},{7,6},{8,7},{9,8},{10,9... | collective-permute-start | bytes 6152 | tf_op jit(solution)/shard_map/ppermute | solution.py:70
  117.9 5.7 %collective-permute-start.13 = (f32[1,2,4,64]{3,2,1,0:T(4,128)S(1)}, f32[1,2,4,64]{3,2,1,0:T(4,128)S(1)}, u32[]{:S(2)}, u32[]{:S(2)}) collective-permute-start(f32[1,2,4,64]{3,2,1,0:T(4,128)S(1)} %collective-permute-done.12), channel_id=1, source_target_pairs={{0,15},{1,0},{2,1},{3,2},{4,3},{5,4},{6,5},{7,6},{8,7},{9,8},{10,9... | collective-permute-start | bytes 6152 | tf_op jit(solution)/shard_map/ppermute | solution.py:70
  123.6 5.7 %collective-permute-start.14 = (f32[1,2,4,64]{3,2,1,0:T(4,128)S(1)}, f32[1,2,4,64]{3,2,1,0:T(4,128)S(1)}, u32[]{:S(2)}, u32[]{:S(2)}) collective-permute-start(f32[1,2,4,64]{3,2,1,0:T(4,128)S(1)} %collective-permute-done.13), channel_id=1, source_target_pairs={{0,15},{1,0},{2,1},{3,2},{4,3},{5,4},{6,5},{7,6},{8,7},{9,8},{10,9... | collective-permute-start | bytes 6152 | tf_op jit(solution)/shard_map/ppermute | solution.py:70
  129.3 5.7 %collective-permute-start.15 = (f32[1,2,4,64]{3,2,1,0:T(4,128)S(1)}, f32[1,2,4,64]{3,2,1,0:T(4,128)S(1)}, u32[]{:S(2)}, u32[]{:S(2)}) collective-permute-start(f32[1,2,4,64]{3,2,1,0:T(4,128)S(1)} %collective-permute-done.14), channel_id=1, source_target_pairs={{0,15},{1,0},{2,1},{3,2},{4,3},{5,4},{6,5},{7,6},{8,7},{9,8},{10,9... | collective-permute-start | bytes 6152 | tf_op jit(solution)/shard_map/ppermute | solution.py:70
  135.1 5.7 %collective-permute-start.16 = (f32[1,2,4,64]{3,2,1,0:T(4,128)S(1)}, f32[1,2,4,64]{3,2,1,0:T(4,128)S(1)}, u32[]{:S(2)}, u32[]{:S(2)}) collective-permute-start(f32[1,2,4,64]{3,2,1,0:T(4,128)S(1)} %collective-permute-done.15), channel_id=1, source_target_pairs={{0,15},{1,0},{2,1},{3,2},{4,3},{5,4},{6,5},{7,6},{8,7},{9,8},{10,9... | collective-permute-start | bytes 6152 | tf_op jit(solution)/shard_map/ppermute | solution.py:70
  221.4 25.3 %collective-permute-start.18 = (bf16[2,4,1,512]{3,1,0,2:T(4,128)(2,1)S(1)}, bf16[2,4,1,512]{3,1,0,2:T(4,128)(2,1)S(1)}, u32[]{:S(2)}, u32[]{:S(2)}) collective-permute-start(bf16[2,4,1,512]{3,1,0,2:T(4,128)(2,1)S(1)} %get-tuple-element.22), channel_id=1, source_target_pairs={{1,0},{2,1},{3,2},{4,3},{5,4},{6,5},{7,6},{8,7},{9,8},{10,9},{11,1... | collective-permute-start | bytes 24584 | tf_op jit(solution)/shard_map/ppermute | solution.py:19
  222.7 12.2 %collective-permute-start.19 = (f32[1,2,4,64]{3,2,1,0:T(4,128)S(1)}, f32[1,2,4,64]{3,2,1,0:T(4,128)S(1)}, u32[]{:S(2)}, u32[]{:S(2)}) collective-permute-start(f32[1,2,4,64]{3,2,1,0:T(4,128)S(1)} %fusion.164), channel_id=1, source_target_pairs={{0,15},{1,0},{2,1},{3,2},{4,3},{5,4},{6,5},{7,6},{8,7},{9,8},{10,9... | collective-permute-start | bytes 6152 | tf_op jit(solution)/shard_map/ppermute | solution.py:70
  232.8 13.8 %collective-permute-start.17 = (bf16[2,4,1,512]{3,1,0,2:T(4,128)(2,1)S(1)}, bf16[2,4,1,512]{3,1,0,2:T(4,128)(2,1)S(1)}, u32[]{:S(2)}, u32[]{:S(2)}) collective-permute-start(bf16[2,4,1,512]{3,1,0,2:T(4,128)(2,1)S(1)} %get-tuple-element.22), channel_id=1, source_target_pairs={{0,1},{1,2},{2,3},{3,4},{4,5},{5,6},{6,7},{7,8},{8,9},{9,10},{10,1... | collective-permute-start | bytes 24584 | tf_op jit(solution)/shard_map/ppermute | solution.py:17
  236.2 5.7 %collective-permute-start.21 = (f32[1,2,4,64]{3,2,1,0:T(4,128)S(1)}, f32[1,2,4,64]{3,2,1,0:T(4,128)S(1)}, u32[]{:S(2)}, u32[]{:S(2)}) collective-permute-start(f32[1,2,4,64]{3,2,1,0:T(4,128)S(1)} %collective-permute-done.20), channel_id=1, source_target_pairs={{0,15},{1,0},{2,1},{3,2},{4,3},{5,4},{6,5},{7,6},{8,7},{9,8},{10,9... | collective-permute-start | bytes 6152 | tf_op jit(solution)/shard_map/ppermute | solution.py:70
  242.0 6.1 %collective-permute-start.22 = (f32[1,2,4,64]{3,2,1,0:T(4,128)S(1)}, f32[1,2,4,64]{3,2,1,0:T(4,128)S(1)}, u32[]{:S(2)}, u32[]{:S(2)}) collective-permute-start(f32[1,2,4,64]{3,2,1,0:T(4,128)S(1)} %collective-permute-done.21), channel_id=1, source_target_pairs={{0,15},{1,0},{2,1},{3,2},{4,3},{5,4},{6,5},{7,6},{8,7},{9,8},{10,9... | collective-permute-start | bytes 6152 | tf_op jit(solution)/shard_map/ppermute | solution.py:70
  253.4 5.7 %collective-permute-start.24 = (f32[1,2,4,64]{3,2,1,0:T(4,128)S(1)}, f32[1,2,4,64]{3,2,1,0:T(4,128)S(1)}, u32[]{:S(2)}, u32[]{:S(2)}) collective-permute-start(f32[1,2,4,64]{3,2,1,0:T(4,128)S(1)} %collective-permute-done.23), channel_id=1, source_target_pairs={{0,15},{1,0},{2,1},{3,2},{4,3},{5,4},{6,5},{7,6},{8,7},{9,8},{10,9... | collective-permute-start | bytes 6152 | tf_op jit(solution)/shard_map/ppermute | solution.py:70
  259.2 5.7 %collective-permute-start.25 = (f32[1,2,4,64]{3,2,1,0:T(4,128)S(1)}, f32[1,2,4,64]{3,2,1,0:T(4,128)S(1)}, u32[]{:S(2)}, u32[]{:S(2)}) collective-permute-start(f32[1,2,4,64]{3,2,1,0:T(4,128)S(1)} %collective-permute-done.24), channel_id=1, source_target_pairs={{0,15},{1,0},{2,1},{3,2},{4,3},{5,4},{6,5},{7,6},{8,7},{9,8},{10,9... | collective-permute-start | bytes 6152 | tf_op jit(solution)/shard_map/ppermute | solution.py:70
  264.9 5.7 %collective-permute-start.26 = (f32[1,2,4,64]{3,2,1,0:T(4,128)S(1)}, f32[1,2,4,64]{3,2,1,0:T(4,128)S(1)}, u32[]{:S(2)}, u32[]{:S(2)}) collective-permute-start(f32[1,2,4,64]{3,2,1,0:T(4,128)S(1)} %collective-permute-done.25), channel_id=1, source_target_pairs={{0,15},{1,0},{2,1},{3,2},{4,3},{5,4},{6,5},{7,6},{8,7},{9,8},{10,9... | collective-permute-start | bytes 6152 | tf_op jit(solution)/shard_map/ppermute | solution.py:70
  270.6 5.7 %collective-permute-start.27 = (f32[1,2,4,64]{3,2,1,0:T(4,128)S(1)}, f32[1,2,4,64]{3,2,1,0:T(4,128)S(1)}, u32[]{:S(2)}, u32[]{:S(2)}) collective-permute-start(f32[1,2,4,64]{3,2,1,0:T(4,128)S(1)} %collective-permute-done.26), channel_id=1, source_target_pairs={{0,15},{1,0},{2,1},{3,2},{4,3},{5,4},{6,5},{7,6},{8,7},{9,8},{10,9... | collective-permute-start | bytes 6152 | tf_op jit(solution)/shard_map/ppermute | solution.py:70
  (13 other events, 359.0 us)
